TPU v7x, 128 devices: a whole 4x4x4 slice. The times are simulated.
128 devices in a mesh: row: 4 (over z_lo, core), col: 8 (over y, z_hi), layer: 4 (over x).
Axes of the slice: x: 4, y: 4, z: 4 (z_hi: 2, z_lo: 2; z = z_hi * 2 + z_lo), core: 2. Of those that a mesh axis runs over, the one named last changes fastest.
Arguments:
- a_tiles: bfloat16 [4, 8, 4, 32, 128, 128], P('row', 'col', 'layer'), may hold values from 0 to 1, as said below
- a_coords: int32 [4, 8, 4, 32, 2], P('row', 'col', 'layer'), may hold values from 0 to 31, as said below
- b_tiles: bfloat16 [4, 8, 4, 32, 128, 128], P('row', 'col', 'layer'), may hold values from 0 to 1, as said below
- b_coords: int32 [4, 8, 4, 32, 2], P('row', 'col', 'layer'), may hold values from 0 to 15, as said below
- out_coords: int32 [4, 8, 4, 16, 2], P('row', 'col', 'layer'), may hold values from 0 to 15, as said below
Outputs:
- flow: float32 [4, 8, 4, 16, 128, 128], P('row', 'col', 'layer')
Inputs may be any that keep to these rules, and one draw needn't show every extreme that they name: `a_tiles`: every entry is positive. `b_tiles`: every entry is positive. `a_coords`: on one device, column 0 takes every value below 32 exactly once; column 1 is below 4. `b_coords`: on one device, column 1 takes every value below 16 exactly twice, with two different values of column 0; column 0 is below 8. `out_coords`: on one device, column 1 takes every value below 16 exactly once; column 0 is below 8.
All inputs are finite; a program needn't handle non-finite values.
Results may differ from a plain program's by a relative error of at most 0.0003.
Values may be sent and summed in bfloat16 or wider, within the bound.
No kernel may reach another device: no remote copies, remote signals or barrier semaphores. Data moves between devices by JAX's collectives and lax.ppermute only.
A program may use at most 192 MiB of HBM per device.

v0:
```python
import jax
import jax.numpy as jnp
from jax import lax
from jax.sharding import PartitionSpec as P

BLK = 4
RB = 4


def local(a_tiles, a_coords, b_tiles, b_coords, out_coords):
    tile_size = a_tiles.shape[-1]
    rows_panel = a_tiles.shape[3]
    col_count = lax.axis_size("col")
    row_count = lax.axis_size("row")
    layer_count = lax.axis_size("layer")
    a_span = BLK
    b_span = BLK * col_count // row_count
    slab_tiles = a_span * col_count
    col_tiles = out_coords.shape[3]
    graph_tiles, graph_coords = (
        lax.all_gather(b_tiles, "row", axis=0, tiled=True),
        lax.all_gather(b_coords, "row", axis=0, tiled=True),
    )
    owner_rows = jnp.arange(row_count, dtype=jnp.int32)[:, None]
    inner_rows = (owner_rows * b_span + graph_coords[:, 0, 0, :, 0]).reshape(-1)
    column_ids = graph_coords[:, 0, 0, :, 1].reshape(-1)
    flat_tiles = graph_tiles.reshape(-1, tile_size, tile_size)
    graph_panel = jnp.zeros((slab_tiles, tile_size, col_tiles, tile_size), jnp.bfloat16)
    graph_panel = graph_panel.at[inner_rows, :, column_ids, :].set(flat_tiles)
    graph_panel = graph_panel.reshape(slab_tiles, tile_size, col_tiles * tile_size)
    own_rows = a_coords[0, 0, 0, :, 0]
    own_inner = a_coords[0, 0, 0, :, 1]
    ordered = jnp.zeros_like(a_tiles[0, 0, 0]).at[own_rows].set(a_tiles[0, 0, 0])
    ordered_inner = jnp.zeros_like(own_inner).at[own_rows].set(own_inner)
    flow_all, inner_all = (
        lax.all_gather(ordered[None], "col", axis=0, tiled=True),
        lax.all_gather(ordered_inner[None], "col", axis=0, tiled=True),
    )
    slab_index = jnp.arange(col_count, dtype=jnp.int32)[:, None] * a_span + inner_all

    def row_block(step_index):
        first_row = step_index * RB
        left_block = lax.dynamic_slice_in_dim(flow_all, first_row, RB, 1)
        index_block = lax.dynamic_slice_in_dim(slab_index, first_row, RB, 1)
        right_block = graph_panel[index_block]
        return jnp.einsum(
            "prxy,pryz->rxz", left_block, right_block, preferred_element_type=jnp.float32
        )

    partial_sum = lax.map(row_block, jnp.arange(rows_panel // RB, dtype=jnp.int32))
    partial_sum = partial_sum.reshape(rows_panel, tile_size, col_tiles * tile_size)
    kept_rows = out_coords[0, 0, 0, :, 0]
    kept_cols = out_coords[0, 0, 0, :, 1]
    summed_rows = lax.psum_scatter(partial_sum, "layer", scatter_dimension=0, tiled=True)
    tile_grid = summed_rows.reshape(b_span, tile_size, col_tiles, tile_size)
    kept_tiles = tile_grid[kept_rows, :, kept_cols, :]
    squared = kept_tiles * kept_tiles
    column_part = jnp.sum(squared, axis=1)
    onehot = (jnp.arange(col_tiles, dtype=jnp.int32)[:, None] == kept_cols[None, :]).astype(
        jnp.float32
    )
    local_mass = jnp.dot(onehot, column_part, precision=lax.Precision.HIGHEST)
    column_total = lax.psum(local_mass, ("row", "layer"))
    factor = jnp.float32(row_count * layer_count * tile_size) / column_total
    flow = squared * factor[kept_cols][:, None, :]
    return flow.reshape(1, 1, 1, col_tiles, tile_size, tile_size)


def solution(mesh):
    in_specs = (
        P("row", "col", "layer", None, None, None),
        P("row", "col", "layer", None, None),
        P("row", "col", "layer", None, None, None),
        P("row", "col", "layer", None, None),
        P("row", "col", "layer", None, None),
    )
    out_specs = P("row", "col", "layer", None, None, None)
    return jax.shard_map(local, mesh=mesh, in_specs=in_specs, out_specs=out_specs, check_vma=False)
```

profile of v0, /device:TPU:0, one launch (start us, length us, event | category | flops | bytes accessed | tf_op | source)
XLA Modules:
  0.0 728.4 jit_solution(13771019656350618229)
XLA Ops:
  6.5 0.7 all-gather.5.cloned.1.call-update
  7.3 0.7 fusion.8
  8.2 3.6 scatter_fusion
  11.8 1.0 copy-done
  12.9 5.3 all_gather.14
  18.5 0.7 slice_bitcast_fusion
  19.2 0.7 scatter_custom_fusion.1
  19.9 1.2 dynamic-slice
  21.7 0.2 dynamic-update-slice
  22.0 13.9 %all-reduce = s32[256]{0:T(256)S(1)} all-reduce(s32[256]{0:T(256)S(1)} %dynamic-update-slice), channel_id=3, replica_groups=mesh['row'=4,'col'=8,'layer'=4] {'col'}, use_global_device_ids=true, to_apply=%add | all-reduce | flops 256 | bytes 2048
  36.0 21.7 %all-gather.5.cloned.1.call-done = bf16[4,1,1,32,128,128]{5,4,3,2,1,0:T(8,128)(2,1)} async-done(((bf16[1,1,1,32,128,128]{5,4,3,2,1,0:T(8,128)(2,1)}), bf16[4,1,1,32,128,128]{5,4,3,2,1,0:T(8,128)(2,1)}) %all-gather.5.cloned.1.call-update) | async-done | bytes 4194320 | tf_op jit(solution)/shard_map/all_gather | solution.py:21
  57.7 6.3 broadcast_in_dim.37
  64.0 21.0 %scatter_fusion.1 = bf16[32,128,16,128]{3,1,2,0:T(8,128)(2,1)} fusion(bf16[32,128,16,128]{3,1,2,0:T(8,128)(2,1)} %broadcast_in_dim.37, s32[128]{0:T(128)S(1)} %fusion.13, bf16[128,128,128]{2,1,0:T(8,128)(2,1)} %bitcast.51), kind=kCustom, calls=%fused_computation.5 | custom fusion | bytes 12583936 | tf_op jit(solution)/shard_map/scatter | solution.py:29
  84.9 22.6 %copy.18 = bf16[32,128,16,128]{1,3,2,0:T(8,128)(2,1)} copy(bf16[32,128,16,128]{3,1,2,0:T(8,128)(2,1)} %scatter_fusion.1) | data formatting | bytes 33554432 | tf_op jit(solution)/shard_map/scatter | solution.py:29
  107.6 22.2 %copy.20 = bf16[32,128,2048]{2,1,0:T(8,128)(2,1)} copy(bf16[32,128,2048]{1,2,0:T(8,128)(2,1)} %bitcast.48) | data formatting | bytes 33554432 | tf_op jit(solution)/shard_map/while | solution.py:50
  129.8 40.7 %all-gather.7.cloned.1.call-done = bf16[256,128,128]{2,1,0:T(8,128)(2,1)} async-done(((bf16[32,128,128]{2,1,0:T(8,128)(2,1)}), bf16[256,128,128]{2,1,0:T(8,128)(2,1)}) %all-gather.7.cloned.1.call-update) | async-done | bytes 8388624 | tf_op jit(solution)/shard_map/all_gather | solution.py:36
  170.5 226.7 %while.10 = (s32[]{:T(128)}, f32[8,4,128,2048]{2,3,1,0:T(8,128)}, s32[8]{0:T(128)S(1)}, bf16[8,32,128,128]{3,2,1,0:T(8,128)(2,1)}, s32[8,32]{1,0:T(8,128)S(1)}, ...) while((s32[]{:T(128)}, f32[8,4,128,2048]{2,3,1,0:T(8,128)}, ...), condition=%wide.region_4.5_spmd, body=%wide.region_3.4_spmd.sunk | while | flops 2147484672 | bytes 55580068 | solution.py:50
  170.5 0.6 dynamic_slice.19
  171.9 13.1 %gather_fusion = bf16[32,128,2048]{2,1,0:T(8,128)(2,1)} fusion(bf16[32,128,2048]{2,1,0:T(8,128)(2,1)} %get-tuple-element.134, s32[1024]{0:T(1024)S(1)} %pad_clamp_fusion.3), kind=kCustom, calls=%fused_computation.clone.1 | custom fusion | bytes 33554560 | tf_op jit(solution)/shard_map/while/body/eval_jaxpr/gather | solution.py:45
  185.0 13.8 %bitcast_dynamic-update-slice_fusion.2 = f32[8,4,128,2048]{2,3,1,0:T(8,128)} fusion(f32[8,4,128,2048]{2,3,1,0:T(8,128)} %get-tuple-element.120, s32[]{:T(128)} %get-tuple-element.119, bf16[8,4,128,2048]{3,2,1,0:T(8,128)(2,1)} %bitcast.47, bf16[8,32,128,128]{3,2,1,0:T(8,128)(2,1)} %get-tuple-element.132, s32[]{:T(128)S(6)} %select_n.95), kind=kOutput, calls=%fused_computation.8.clone.1 | convolution fusion | flops 2147483648 | bytes 22020612 | tf_op jit(solution)/shard_map/while/body/eval_jaxpr/prxy,pryz->rxz/dot_general | solution.py:46
  198.8 0.6 dynamic_slice.19
  200.2 13.1 %gather_fusion = bf16[32,128,2048]{2,1,0:T(8,128)(2,1)} fusion(bf16[32,128,2048]{2,1,0:T(8,128)(2,1)} %get-tuple-element.134, s32[1024]{0:T(1024)S(1)} %pad_clamp_fusion.3), kind=kCustom, calls=%fused_computation.clone.1 | custom fusion | bytes 33554560 | tf_op jit(solution)/shard_map/while/body/eval_jaxpr/gather | solution.py:45
  213.3 13.8 %bitcast_dynamic-update-slice_fusion.2 = f32[8,4,128,2048]{2,3,1,0:T(8,128)} fusion(f32[8,4,128,2048]{2,3,1,0:T(8,128)} %get-tuple-element.120, s32[]{:T(128)} %get-tuple-element.119, bf16[8,4,128,2048]{3,2,1,0:T(8,128)(2,1)} %bitcast.47, bf16[8,32,128,128]{3,2,1,0:T(8,128)(2,1)} %get-tuple-element.132, s32[]{:T(128)S(6)} %select_n.95), kind=kOutput, calls=%fused_computation.8.clone.1 | convolution fusion | flops 2147483648 | bytes 22020612 | tf_op jit(solution)/shard_map/while/body/eval_jaxpr/prxy,pryz->rxz/dot_general | solution.py:46
  227.1 0.6 dynamic_slice.19
  228.5 13.1 %gather_fusion = bf16[32,128,2048]{2,1,0:T(8,128)(2,1)} fusion(bf16[32,128,2048]{2,1,0:T(8,128)(2,1)} %get-tuple-element.134, s32[1024]{0:T(1024)S(1)} %pad_clamp_fusion.3), kind=kCustom, calls=%fused_computation.clone.1 | custom fusion | bytes 33554560 | tf_op jit(solution)/shard_map/while/body/eval_jaxpr/gather | solution.py:45
  241.7 13.8 %bitcast_dynamic-update-slice_fusion.2 = f32[8,4,128,2048]{2,3,1,0:T(8,128)} fusion(f32[8,4,128,2048]{2,3,1,0:T(8,128)} %get-tuple-element.120, s32[]{:T(128)} %get-tuple-element.119, bf16[8,4,128,2048]{3,2,1,0:T(8,128)(2,1)} %bitcast.47, bf16[8,32,128,128]{3,2,1,0:T(8,128)(2,1)} %get-tuple-element.132, s32[]{:T(128)S(6)} %select_n.95), kind=kOutput, calls=%fused_computation.8.clone.1 | convolution fusion | flops 2147483648 | bytes 22020612 | tf_op jit(solution)/shard_map/while/body/eval_jaxpr/prxy,pryz->rxz/dot_general | solution.py:46
  255.5 0.6 dynamic_slice.19
  256.9 13.1 %gather_fusion = bf16[32,128,2048]{2,1,0:T(8,128)(2,1)} fusion(bf16[32,128,2048]{2,1,0:T(8,128)(2,1)} %get-tuple-element.134, s32[1024]{0:T(1024)S(1)} %pad_clamp_fusion.3), kind=kCustom, calls=%fused_computation.clone.1 | custom fusion | bytes 33554560 | tf_op jit(solution)/shard_map/while/body/eval_jaxpr/gather | solution.py:45
  270.0 13.8 %bitcast_dynamic-update-slice_fusion.2 = f32[8,4,128,2048]{2,3,1,0:T(8,128)} fusion(f32[8,4,128,2048]{2,3,1,0:T(8,128)} %get-tuple-element.120, s32[]{:T(128)} %get-tuple-element.119, bf16[8,4,128,2048]{3,2,1,0:T(8,128)(2,1)} %bitcast.47, bf16[8,32,128,128]{3,2,1,0:T(8,128)(2,1)} %get-tuple-element.132, s32[]{:T(128)S(6)} %select_n.95), kind=kOutput, calls=%fused_computation.8.clone.1 | convolution fusion | flops 2147483648 | bytes 22020612 | tf_op jit(solution)/shard_map/while/body/eval_jaxpr/prxy,pryz->rxz/dot_general | solution.py:46
  283.8 0.6 dynamic_slice.19
  285.2 13.1 %gather_fusion = bf16[32,128,2048]{2,1,0:T(8,128)(2,1)} fusion(bf16[32,128,2048]{2,1,0:T(8,128)(2,1)} %get-tuple-element.134, s32[1024]{0:T(1024)S(1)} %pad_clamp_fusion.3), kind=kCustom, calls=%fused_computation.clone.1 | custom fusion | bytes 33554560 | tf_op jit(solution)/shard_map/while/body/eval_jaxpr/gather | solution.py:45
  298.4 13.8 %bitcast_dynamic-update-slice_fusion.2 = f32[8,4,128,2048]{2,3,1,0:T(8,128)} fusion(f32[8,4,128,2048]{2,3,1,0:T(8,128)} %get-tuple-element.120, s32[]{:T(128)} %get-tuple-element.119, bf16[8,4,128,2048]{3,2,1,0:T(8,128)(2,1)} %bitcast.47, bf16[8,32,128,128]{3,2,1,0:T(8,128)(2,1)} %get-tuple-element.132, s32[]{:T(128)S(6)} %select_n.95), kind=kOutput, calls=%fused_computation.8.clone.1 | convolution fusion | flops 2147483648 | bytes 22020612 | tf_op jit(solution)/shard_map/while/body/eval_jaxpr/prxy,pryz->rxz/dot_general | solution.py:46
  312.1 0.6 dynamic_slice.19
  313.5 13.1 %gather_fusion = bf16[32,128,2048]{2,1,0:T(8,128)(2,1)} fusion(bf16[32,128,2048]{2,1,0:T(8,128)(2,1)} %get-tuple-element.134, s32[1024]{0:T(1024)S(1)} %pad_clamp_fusion.3), kind=kCustom, calls=%fused_computation.clone.1 | custom fusion | bytes 33554560 | tf_op jit(solution)/shard_map/while/body/eval_jaxpr/gather | solution.py:45
  326.7 13.8 %bitcast_dynamic-update-slice_fusion.2 = f32[8,4,128,2048]{2,3,1,0:T(8,128)} fusion(f32[8,4,128,2048]{2,3,1,0:T(8,128)} %get-tuple-element.120, s32[]{:T(128)} %get-tuple-element.119, bf16[8,4,128,2048]{3,2,1,0:T(8,128)(2,1)} %bitcast.47, bf16[8,32,128,128]{3,2,1,0:T(8,128)(2,1)} %get-tuple-element.132, s32[]{:T(128)S(6)} %select_n.95), kind=kOutput, calls=%fused_computation.8.clone.1 | convolution fusion | flops 2147483648 | bytes 22020612 | tf_op jit(solution)/shard_map/while/body/eval_jaxpr/prxy,pryz->rxz/dot_general | solution.py:46
  340.5 0.6 dynamic_slice.19
  341.9 13.1 %gather_fusion = bf16[32,128,2048]{2,1,0:T(8,128)(2,1)} fusion(bf16[32,128,2048]{2,1,0:T(8,128)(2,1)} %get-tuple-element.134, s32[1024]{0:T(1024)S(1)} %pad_clamp_fusion.3), kind=kCustom, calls=%fused_computation.clone.1 | custom fusion | bytes 33554560 | tf_op jit(solution)/shard_map/while/body/eval_jaxpr/gather | solution.py:45
  355.0 13.8 %bitcast_dynamic-update-slice_fusion.2 = f32[8,4,128,2048]{2,3,1,0:T(8,128)} fusion(f32[8,4,128,2048]{2,3,1,0:T(8,128)} %get-tuple-element.120, s32[]{:T(128)} %get-tuple-element.119, bf16[8,4,128,2048]{3,2,1,0:T(8,128)(2,1)} %bitcast.47, bf16[8,32,128,128]{3,2,1,0:T(8,128)(2,1)} %get-tuple-element.132, s32[]{:T(128)S(6)} %select_n.95), kind=kOutput, calls=%fused_computation.8.clone.1 | convolution fusion | flops 2147483648 | bytes 22020612 | tf_op jit(solution)/shard_map/while/body/eval_jaxpr/prxy,pryz->rxz/dot_general | solution.py:46
  368.9 0.6 dynamic_slice.19
  370.3 13.1 %gather_fusion = bf16[32,128,2048]{2,1,0:T(8,128)(2,1)} fusion(bf16[32,128,2048]{2,1,0:T(8,128)(2,1)} %get-tuple-element.134, s32[1024]{0:T(1024)S(1)} %pad_clamp_fusion.3), kind=kCustom, calls=%fused_computation.clone.1 | custom fusion | bytes 33554560 | tf_op jit(solution)/shard_map/while/body/eval_jaxpr/gather | solution.py:45
  383.4 13.8 %bitcast_dynamic-update-slice_fusion.2 = f32[8,4,128,2048]{2,3,1,0:T(8,128)} fusion(f32[8,4,128,2048]{2,3,1,0:T(8,128)} %get-tuple-element.120, s32[]{:T(128)} %get-tuple-element.119, bf16[8,4,128,2048]{3,2,1,0:T(8,128)(2,1)} %bitcast.47, bf16[8,32,128,128]{3,2,1,0:T(8,128)(2,1)} %get-tuple-element.132, s32[]{:T(128)S(6)} %select_n.95), kind=kOutput, calls=%fused_computation.8.clone.1 | convolution fusion | flops 2147483648 | bytes 22020612 | tf_op jit(solution)/shard_map/while/body/eval_jaxpr/prxy,pryz->rxz/dot_general | solution.py:46
  397.2 0.7 copy-done.1
  397.9 279.9 %reduce-scatter.2.cloned.1.call-done = f32[8,128,2048]{1,2,0:T(8,128)} async-done(((f32[32,128,2048]{1,2,0:T(8,128)}), f32[8,128,2048]{1,2,0:T(8,128)}) %reduce-scatter.2.cloned.1.call-update) | async-done | bytes 8388624 | tf_op jit(solution)/shard_map/reduce_scatter | solution.py:54
  677.8 9.1 %copy.22 = f32[8,128,16,128]{3,1,2,0:T(8,128)} copy(f32[8,128,16,128]{1,3,2,0:T(8,128)} %bitcast.50) | data formatting | bytes 16777216 | tf_op jit(solution)/shard_map/reshape | solution.py:55
  686.9 4.0 gather_fusion.1
  691.1 29.0 %psum.7 = f32[16,128]{1,0:T(8,128)S(1)} all-reduce(f32[16,128]{1,0:T(8,128)S(1)} %fusion.5), channel_id=1, replica_groups=mesh['row'=4,'col'=8,'layer'=4] {'row','layer'}, use_global_device_ids=true, to_apply=%region_7.8 | all-reduce | flops 2048 | bytes 16384 | tf_op jit(solution)/shard_map/psum | solution.py:63
  720.2 0.6 gather_fusion.2
  720.7 1.1 bitcast_multiply_fusion
  (51 shorter events, 2.4 us)
Async XLA Ops:
  6.5 51.1 %all-gather.5.cloned.1.call-start = ((), (), s32[]{:S(2)}) async-start(), calls=%async_computation.1 | async-start | bytes 5242880 | tf_op jit(solution)/shard_map/all_gather | solution.py:21
  7.3 163.2 %all-gather.7.cloned.1.call-start = ((), (), s32[]{:S(2)}) async-start(), calls=%async_computation.3 | async-start | bytes 9437184 | tf_op jit(solution)/shard_map/all_gather | solution.py:36
  11.8 1.0 copy-start
  12.8 665.0 %reduce-scatter.2.cloned.1.call-start = ((), (), s32[]{:S(2)}) async-start(), calls=%async_computation.2 | async-start | bytes 41943040 | tf_op jit(solution)/shard_map/reduce_scatter | solution.py:54
  397.2 0.7 copy-start.1
Sparse Core Ops, SparseCore 0:
  9.0 48.6 all-gather.4
  60.0 110.3 all-gather.6
  397.3 280.3 reduce-scatter.1
where the time goes:
time: 731 us; the launch traced here: 728 us
  waiting for transfers between devices  343 us (47%)
  local copies, waits for them, and re-layouts  205 us (28%)
  matrix products  111 us (15%)
  blocking collectives  48.2 us (7%)
  between operations  13.8 us (2%)
    reduce_scatter x1, waiting for transfers between devices, local(): lax.psum_scatter(partial_sum, 'layer', scatter_dimension=0, tiled=True)  280 us
    dot_general x8, matrix products, row_block(): jnp.einsum('prxy,pryz->rxz', left_block, right_block, preferred_element_t...  110 us
    gather x8, local copies, waits for them, and re-layouts, row_block(): right_block = graph_panel[index_block]  105 us
    scatter x2, local copies, waits for them, and re-layouts, local(): graph_panel = graph_panel.at[inner_rows, :, column_ids, :].set(flat_tiles)  43.6 us
    all_gather x1, waiting for transfers between devices, local(): lax.all_gather(ordered[None], 'col', axis=0, tiled=True)  40.7 us
    psum x1, blocking collectives, local(): column_total = lax.psum(local_mass, ('row', 'layer'))  29 us
    while x1, local copies, waits for them, and re-layouts, local(): lax.map(row_block, jnp.arange(rows_panel // RB, dtype=jnp.int32))  22.2 us
    all_gather x1, waiting for transfers between devices, local(): lax.all_gather(b_tiles, 'row', axis=0, tiled=True)  21.7 us
  transfers between devices with their start and end apart: 3, of which 3 were waited for; matrix products, arithmetic and copies ran while one was open for 11% of the time, Pallas kernels for 0%

commit v1 on v0

--- a/solution.py
+++ b/solution.py
@@ -33,7 +33,9 @@
     ordered = jnp.zeros_like(a_tiles[0, 0, 0]).at[own_rows].set(a_tiles[0, 0, 0])
     ordered_inner = jnp.zeros_like(own_inner).at[own_rows].set(own_inner)
     flow_all, inner_all = (
-        lax.all_gather(ordered[None], "col", axis=0, tiled=True),
+        jnp.concatenate(
+            lax.all_to_all(jnp.stack([ordered[None]] * lax.axis_size("col")), "col", 0, 0), axis=0
+        ),
         lax.all_gather(ordered_inner[None], "col", axis=0, tiled=True),
     )
     slab_index = jnp.arange(col_count, dtype=jnp.int32)[:, None] * a_span + inner_all

time: 731 us -> 789 us (1.079)
  blocking collectives: 48.2 us -> 157 us
  waiting for transfers between devices: 343 us -> 282 us
    all_gather x1, blocking collectives: 5.32 us -> 114 us  [local(): lax.all_gather(b_coords, 'row', axis=0, tiled=True)]
    all_gather x1 -> x0, waiting for transfers between devices: 40.7 us -> none  [local(): lax.all_gather(ordered[None], 'col', axis=0, tiled=True)]
    all_gather x1, waiting for transfers between devices: 21.7 us -> 0.01 us  [local(): lax.all_gather(b_tiles, 'row', axis=0, tiled=True)]
  transfers between devices with their start and end apart: 3 -> 3, of which waited for: 3 -> 1; matrix products, arithmetic and copies ran while one was open for 11% -> 9% of each run, Pallas kernels for 0% -> 0%
where the time goes in v1:
time: 789 us; the launch traced here: 787 us
  waiting for transfers between devices  282 us (36%)
  local copies, waits for them, and re-layouts  208 us (26%)
  blocking collectives  157 us (20%)
  matrix products  111 us (14%)
  between operations  14.1 us (2%)
  starting transfers between devices  7.94 us (1%)
    reduce_scatter x1, waiting for transfers between devices, local(): lax.psum_scatter(partial_sum, 'layer', scatter_dimension=0, tiled=True)  282 us
    all_gather x1, blocking collectives, local(): lax.all_gather(b_coords, 'row', axis=0, tiled=True)  114 us
    dot_general x8, matrix products, row_block(): jnp.einsum('prxy,pryz->rxz', left_block, right_block, preferred_element_t...  110 us
    gather x8, local copies, waits for them, and re-layouts, row_block(): right_block = graph_panel[index_block]  105 us
    scatter x2, local copies, waits for them, and re-layouts, local(): graph_panel = graph_panel.at[inner_rows, :, column_ids, :].set(flat_tiles)  43.3 us
    psum x1, blocking collectives, local(): column_total = lax.psum(local_mass, ('row', 'layer'))  29 us
    while x1, local copies, waits for them, and re-layouts, local(): lax.map(row_block, jnp.arange(rows_panel // RB, dtype=jnp.int32))  22.2 us
  transfers between devices with their start and end apart: 3, of which 1 were waited for; matrix products, arithmetic and copies ran while one was open for 9% of the time, Pallas kernels for 0%

profile of v1, /device:TPU:0, one launch (start us, length us, event | category | flops | bytes accessed | tf_op | source)
XLA Modules:
  0.0 786.8 jit_solution(3279142669488154325)
XLA Ops:
  6.5 0.8 fusion.8
  7.3 0.2 broadcast_in_dim.16
  7.5 3.6 scatter_fusion
  11.1 5.4 stack.3
  16.5 7.9 all-to-all-start
  24.4 0.7 all-gather.3.cloned.1.call-update
  25.2 113.9 %all_gather.10 = s32[4,1,1,32,2]{3,4,2,1,0:T(2,128)S(1)} all-gather(s32[1,1,1,32,2]{3,4,2,1,0:T(2,128)S(1)} %copy-done), channel_id=1, replica_groups=mesh['row'=4,'col'=8,'layer'=4] {'row'}, dimensions={0}, use_global_device_ids=true | all-gather | bytes 1280 | tf_op jit(solution)/shard_map/all_gather | solution.py:22
  139.5 0.7 scatter_custom_fusion.1
  140.2 0.6 dynamic-slice
  141.3 0.2 dynamic-update-slice
  141.6 13.6 %all-reduce = s32[256]{0:T(256)S(1)} all-reduce(s32[256]{0:T(256)S(1)} %dynamic-update-slice), channel_id=2, replica_groups=mesh['row'=4,'col'=8,'layer'=4] {'col'}, use_global_device_ids=true, to_apply=%add | all-reduce | flops 256 | bytes 2048
  155.3 6.3 broadcast_in_dim.18
  161.6 20.8 %scatter_fusion.1 = bf16[32,128,16,128]{3,1,2,0:T(8,128)(2,1)} fusion(bf16[32,128,16,128]{3,1,2,0:T(8,128)(2,1)} %broadcast_in_dim.18, s32[128]{0:T(128)S(1)} %fusion.13, bf16[128,128,128]{2,1,0:T(8,128)(2,1)} %bitcast.51), kind=kCustom, calls=%fused_computation.5 | custom fusion | bytes 12583936 | tf_op jit(solution)/shard_map/scatter | solution.py:29
  182.4 22.5 %copy.16 = bf16[32,128,16,128]{1,3,2,0:T(8,128)(2,1)} copy(bf16[32,128,16,128]{3,1,2,0:T(8,128)(2,1)} %scatter_fusion.1) | data formatting | bytes 33554432 | tf_op jit(solution)/shard_map/scatter | solution.py:29
  204.9 22.2 %copy.18 = bf16[32,128,2048]{2,1,0:T(8,128)(2,1)} copy(bf16[32,128,2048]{1,2,0:T(8,128)(2,1)} %bitcast.48) | data formatting | bytes 33554432 | tf_op jit(solution)/shard_map/while | solution.py:52
  227.1 226.6 %while.10 = (s32[]{:T(128)}, f32[8,4,128,2048]{2,3,1,0:T(8,128)}, s32[8]{0:T(128)S(1)}, bf16[8,32,128,128]{3,2,1,0:T(8,128)(2,1)}, s32[8,32]{1,0:T(8,128)S(1)}, ...) while((s32[]{:T(128)}, f32[8,4,128,2048]{2,3,1,0:T(8,128)}, ...), condition=%wide.region_4.5_spmd, body=%wide.region_3.4_spmd.sunk | while | flops 2147484672 | bytes 55580068 | solution.py:52
  227.1 0.6 dynamic_slice.19
  228.5 13.1 %gather_fusion = bf16[32,128,2048]{2,1,0:T(8,128)(2,1)} fusion(bf16[32,128,2048]{2,1,0:T(8,128)(2,1)} %get-tuple-element.134, s32[1024]{0:T(1024)S(1)} %pad_clamp_fusion.3), kind=kCustom, calls=%fused_computation.clone.1 | custom fusion | bytes 33554560 | tf_op jit(solution)/shard_map/while/body/eval_jaxpr/gather | solution.py:47
  241.6 13.8 %bitcast_dynamic-update-slice_fusion.2 = f32[8,4,128,2048]{2,3,1,0:T(8,128)} fusion(f32[8,4,128,2048]{2,3,1,0:T(8,128)} %get-tuple-element.120, s32[]{:T(128)} %get-tuple-element.119, bf16[8,4,128,2048]{3,2,1,0:T(8,128)(2,1)} %bitcast.47, bf16[8,32,128,128]{3,2,1,0:T(8,128)(2,1)} %get-tuple-element.132, s32[]{:T(128)S(6)} %select_n.95), kind=kOutput, calls=%fused_computation.8.clone.1 | convolution fusion | flops 2147483648 | bytes 22020612 | tf_op jit(solution)/shard_map/while/body/eval_jaxpr/prxy,pryz->rxz/dot_general | solution.py:48
  255.4 0.6 dynamic_slice.19
  256.8 13.1 %gather_fusion = bf16[32,128,2048]{2,1,0:T(8,128)(2,1)} fusion(bf16[32,128,2048]{2,1,0:T(8,128)(2,1)} %get-tuple-element.134, s32[1024]{0:T(1024)S(1)} %pad_clamp_fusion.3), kind=kCustom, calls=%fused_computation.clone.1 | custom fusion | bytes 33554560 | tf_op jit(solution)/shard_map/while/body/eval_jaxpr/gather | solution.py:47
  269.9 13.8 %bitcast_dynamic-update-slice_fusion.2 = f32[8,4,128,2048]{2,3,1,0:T(8,128)} fusion(f32[8,4,128,2048]{2,3,1,0:T(8,128)} %get-tuple-element.120, s32[]{:T(128)} %get-tuple-element.119, bf16[8,4,128,2048]{3,2,1,0:T(8,128)(2,1)} %bitcast.47, bf16[8,32,128,128]{3,2,1,0:T(8,128)(2,1)} %get-tuple-element.132, s32[]{:T(128)S(6)} %select_n.95), kind=kOutput, calls=%fused_computation.8.clone.1 | convolution fusion | flops 2147483648 | bytes 22020612 | tf_op jit(solution)/shard_map/while/body/eval_jaxpr/prxy,pryz->rxz/dot_general | solution.py:48
  283.8 0.6 dynamic_slice.19
  285.1 13.1 %gather_fusion = bf16[32,128,2048]{2,1,0:T(8,128)(2,1)} fusion(bf16[32,128,2048]{2,1,0:T(8,128)(2,1)} %get-tuple-element.134, s32[1024]{0:T(1024)S(1)} %pad_clamp_fusion.3), kind=kCustom, calls=%fused_computation.clone.1 | custom fusion | bytes 33554560 | tf_op jit(solution)/shard_map/while/body/eval_jaxpr/gather | solution.py:47
  298.3 13.8 %bitcast_dynamic-update-slice_fusion.2 = f32[8,4,128,2048]{2,3,1,0:T(8,128)} fusion(f32[8,4,128,2048]{2,3,1,0:T(8,128)} %get-tuple-element.120, s32[]{:T(128)} %get-tuple-element.119, bf16[8,4,128,2048]{3,2,1,0:T(8,128)(2,1)} %bitcast.47, bf16[8,32,128,128]{3,2,1,0:T(8,128)(2,1)} %get-tuple-element.132, s32[]{:T(128)S(6)} %select_n.95), kind=kOutput, calls=%fused_computation.8.clone.1 | convolution fusion | flops 2147483648 | bytes 22020612 | tf_op jit(solution)/shard_map/while/body/eval_jaxpr/prxy,pryz->rxz/dot_general | solution.py:48
  312.1 0.6 dynamic_slice.19
  313.5 13.1 %gather_fusion = bf16[32,128,2048]{2,1,0:T(8,128)(2,1)} fusion(bf16[32,128,2048]{2,1,0:T(8,128)(2,1)} %get-tuple-element.134, s32[1024]{0:T(1024)S(1)} %pad_clamp_fusion.3), kind=kCustom, calls=%fused_computation.clone.1 | custom fusion | bytes 33554560 | tf_op jit(solution)/shard_map/while/body/eval_jaxpr/gather | solution.py:47
  326.6 13.8 %bitcast_dynamic-update-slice_fusion.2 = f32[8,4,128,2048]{2,3,1,0:T(8,128)} fusion(f32[8,4,128,2048]{2,3,1,0:T(8,128)} %get-tuple-element.120, s32[]{:T(128)} %get-tuple-element.119, bf16[8,4,128,2048]{3,2,1,0:T(8,128)(2,1)} %bitcast.47, bf16[8,32,128,128]{3,2,1,0:T(8,128)(2,1)} %get-tuple-element.132, s32[]{:T(128)S(6)} %select_n.95), kind=kOutput, calls=%fused_computation.8.clone.1 | convolution fusion | flops 2147483648 | bytes 22020612 | tf_op jit(solution)/shard_map/while/body/eval_jaxpr/prxy,pryz->rxz/dot_general | solution.py:48
  340.4 0.6 dynamic_slice.19
  341.8 13.1 %gather_fusion = bf16[32,128,2048]{2,1,0:T(8,128)(2,1)} fusion(bf16[32,128,2048]{2,1,0:T(8,128)(2,1)} %get-tuple-element.134, s32[1024]{0:T(1024)S(1)} %pad_clamp_fusion.3), kind=kCustom, calls=%fused_computation.clone.1 | custom fusion | bytes 33554560 | tf_op jit(solution)/shard_map/while/body/eval_jaxpr/gather | solution.py:47
  355.0 13.8 %bitcast_dynamic-update-slice_fusion.2 = f32[8,4,128,2048]{2,3,1,0:T(8,128)} fusion(f32[8,4,128,2048]{2,3,1,0:T(8,128)} %get-tuple-element.120, s32[]{:T(128)} %get-tuple-element.119, bf16[8,4,128,2048]{3,2,1,0:T(8,128)(2,1)} %bitcast.47, bf16[8,32,128,128]{3,2,1,0:T(8,128)(2,1)} %get-tuple-element.132, s32[]{:T(128)S(6)} %select_n.95), kind=kOutput, calls=%fused_computation.8.clone.1 | convolution fusion | flops 2147483648 | bytes 22020612 | tf_op jit(solution)/shard_map/while/body/eval_jaxpr/prxy,pryz->rxz/dot_general | solution.py:48
  368.7 0.6 dynamic_slice.19
  370.1 13.1 %gather_fusion = bf16[32,128,2048]{2,1,0:T(8,128)(2,1)} fusion(bf16[32,128,2048]{2,1,0:T(8,128)(2,1)} %get-tuple-element.134, s32[1024]{0:T(1024)S(1)} %pad_clamp_fusion.3), kind=kCustom, calls=%fused_computation.clone.1 | custom fusion | bytes 33554560 | tf_op jit(solution)/shard_map/while/body/eval_jaxpr/gather | solution.py:47
  383.2 13.8 %bitcast_dynamic-update-slice_fusion.2 = f32[8,4,128,2048]{2,3,1,0:T(8,128)} fusion(f32[8,4,128,2048]{2,3,1,0:T(8,128)} %get-tuple-element.120, s32[]{:T(128)} %get-tuple-element.119, bf16[8,4,128,2048]{3,2,1,0:T(8,128)(2,1)} %bitcast.47, bf16[8,32,128,128]{3,2,1,0:T(8,128)(2,1)} %get-tuple-element.132, s32[]{:T(128)S(6)} %select_n.95), kind=kOutput, calls=%fused_computation.8.clone.1 | convolution fusion | flops 2147483648 | bytes 22020612 | tf_op jit(solution)/shard_map/while/body/eval_jaxpr/prxy,pryz->rxz/dot_general | solution.py:48
  397.1 0.6 dynamic_slice.19
  398.4 13.1 %gather_fusion = bf16[32,128,2048]{2,1,0:T(8,128)(2,1)} fusion(bf16[32,128,2048]{2,1,0:T(8,128)(2,1)} %get-tuple-element.134, s32[1024]{0:T(1024)S(1)} %pad_clamp_fusion.3), kind=kCustom, calls=%fused_computation.clone.1 | custom fusion | bytes 33554560 | tf_op jit(solution)/shard_map/while/body/eval_jaxpr/gather | solution.py:47
  411.6 13.8 %bitcast_dynamic-update-slice_fusion.2 = f32[8,4,128,2048]{2,3,1,0:T(8,128)} fusion(f32[8,4,128,2048]{2,3,1,0:T(8,128)} %get-tuple-element.120, s32[]{:T(128)} %get-tuple-element.119, bf16[8,4,128,2048]{3,2,1,0:T(8,128)(2,1)} %bitcast.47, bf16[8,32,128,128]{3,2,1,0:T(8,128)(2,1)} %get-tuple-element.132, s32[]{:T(128)S(6)} %select_n.95), kind=kOutput, calls=%fused_computation.8.clone.1 | convolution fusion | flops 2147483648 | bytes 22020612 | tf_op jit(solution)/shard_map/while/body/eval_jaxpr/prxy,pryz->rxz/dot_general | solution.py:48
  425.4 0.6 dynamic_slice.19
  426.8 13.1 %gather_fusion = bf16[32,128,2048]{2,1,0:T(8,128)(2,1)} fusion(bf16[32,128,2048]{2,1,0:T(8,128)(2,1)} %get-tuple-element.134, s32[1024]{0:T(1024)S(1)} %pad_clamp_fusion.3), kind=kCustom, calls=%fused_computation.clone.1 | custom fusion | bytes 33554560 | tf_op jit(solution)/shard_map/while/body/eval_jaxpr/gather | solution.py:47
  439.9 13.8 %bitcast_dynamic-update-slice_fusion.2 = f32[8,4,128,2048]{2,3,1,0:T(8,128)} fusion(f32[8,4,128,2048]{2,3,1,0:T(8,128)} %get-tuple-element.120, s32[]{:T(128)} %get-tuple-element.119, bf16[8,4,128,2048]{3,2,1,0:T(8,128)(2,1)} %bitcast.47, bf16[8,32,128,128]{3,2,1,0:T(8,128)(2,1)} %get-tuple-element.132, s32[]{:T(128)S(6)} %select_n.95), kind=kOutput, calls=%fused_computation.8.clone.1 | convolution fusion | flops 2147483648 | bytes 22020612 | tf_op jit(solution)/shard_map/while/body/eval_jaxpr/prxy,pryz->rxz/dot_general | solution.py:48
  453.7 0.7 copy-done.1
  454.4 281.5 %reduce-scatter.2.cloned.1.call-done = f32[8,128,2048]{1,2,0:T(8,128)} async-done(((f32[32,128,2048]{1,2,0:T(8,128)}), f32[8,128,2048]{1,2,0:T(8,128)}) %reduce-scatter.2.cloned.1.call-update) | async-done | bytes 8388624 | tf_op jit(solution)/shard_map/reduce_scatter | solution.py:56
  735.9 9.1 %copy.20 = f32[8,128,16,128]{3,1,2,0:T(8,128)} copy(f32[8,128,16,128]{1,3,2,0:T(8,128)} %bitcast.50) | data formatting | bytes 16777216 | tf_op jit(solution)/shard_map/reshape | solution.py:57
  745.1 4.0 gather_fusion.1
  749.2 0.1 fusion.5
  749.3 29.0 %psum.7 = f32[16,128]{1,0:T(8,128)S(1)} all-reduce(f32[16,128]{1,0:T(8,128)S(1)} %fusion.5), channel_id=1, replica_groups=mesh['row'=4,'col'=8,'layer'=4] {'row','layer'}, use_global_device_ids=true, to_apply=%region_7.8 | all-reduce | flops 2048 | bytes 16384 | tf_op jit(solution)/shard_map/psum | solution.py:65
  778.3 0.6 gather_fusion.2
  778.9 1.1 bitcast_multiply_fusion
  (55 shorter events, 2.1 us)
Async XLA Ops:
  6.5 133.6 %copy-start.3 = (u32[128]{0:T(128)S(1)}, u32[128]{0:T(128)}, u32[]{:S(2)}) copy-start(u32[128]{0:T(128)} %constant.75) | copy-start | bytes 1540
  6.5 132.9 %copy-start.2 = (s32[1,1,1,32,2]{3,4,2,1,0:T(2,128)S(1)}, s32[1,1,1,32,2]{3,4,2,1,0:T(2,128)}, u32[]{:S(2)}) copy-start(s32[1,1,1,32,2]{3,4,2,1,0:T(2,128)} %param.8) | copy-start | bytes 772
  6.5 18.7 %copy-start = (s32[1,1,1,32,2]{3,4,2,1,0:T(2,128)S(1)}, s32[1,1,1,32,2]{3,4,2,1,0:T(2,128)}, u32[]{:S(2)}) copy-start(s32[1,1,1,32,2]{3,4,2,1,0:T(2,128)} %param.10) | copy-start | bytes 772
  16.5 210.6 %all-to-all-start = ((bf16[8,1,32,128,128]{4,3,2,1,0:T(8,128)(2,1)}), bf16[8,1,32,128,128]{4,3,2,1,0:T(8,128)(2,1)}, u32[]{:S(2)}, u32[]{:S(2)}) async-start(bf16[8,1,32,128,128]{4,3,2,1,0:T(8,128)(2,1)} %stack.3), calls=%async_computation | async-start | bytes 16777216 | tf_op jit(solution)/shard_map/all_to_all | solution.py:37
  24.4 130.9 %all-gather.3.cloned.1.call-start = ((), (), s32[]{:S(2)}) async-start(), calls=%async_computation.2 | async-start | bytes 5242880 | tf_op jit(solution)/shard_map/all_gather | solution.py:21
  25.1 710.8 %reduce-scatter.2.cloned.1.call-start = ((), (), s32[]{:S(2)}) async-start(), calls=%async_computation.3 | async-start | bytes 41943040 | tf_op jit(solution)/shard_map/reduce_scatter | solution.py:56
  453.7 0.7 copy-start.1
Sparse Core Ops, SparseCore 0:
  26.9 123.0 all-gather.2
  453.9 282.0 reduce-scatter.1
